TPU v7x, 32 devices: a whole 2x2x4 slice. The times are simulated.
32 devices in a mesh: gx: 4 (over z), gy: 2 (over y), gz: 4 (over x, core).
Axes of the slice: x: 2, y: 2, z: 4, core: 2. Of those that a mesh axis runs over, the one named last changes fastest.
Arguments:
- positions: float32 [3, 4, 2, 8, 128], P(None, 'gx', 'gy', 'gz'), may hold values from 0 to 8, as said below
- velocity: float32 [3, 4, 2, 8, 128], P(None, 'gx', 'gy', 'gz'), may hold values from -16 to 16
- counts: int32 [4, 2, 8], P('gx', 'gy', 'gz'), may hold values from 0 to 128, as said below
Outputs:
- velocity_new: float32 [3, 4, 2, 8, 128], P(None, 'gx', 'gy', 'gz')
- pressure: float32 [4, 2, 8, 128], P('gx', 'gy', 'gz')
Inputs may be any that keep to these rules, and one draw needn't show every extreme that they name: `positions`: component k of the position of any slot of tile (a, b, c) lies in [t, t + 1), where t is a, b or c for k = 0, 1, 2. A tile's particles fill its first counts[a, b, c] slots. In every column of tiles the bottom tile is full, the tiles below one topmost wet tile hold 96 or more particles, and the tiles above it are empty.
All inputs are finite; a program needn't handle non-finite values.
Results may differ from a plain program's by a relative error of at most 0.0003.
Values sent between devices are 32-bit elements; how exact they have to be, the bound alone decides.
No kernel may reach another device: no remote copies, remote signals or barrier semaphores. Data moves between devices by JAX's collectives and lax.ppermute only.
A program may use at most 64 MiB of HBM per device.

v0:
```python
import jax
import jax.numpy as jnp
from jax import lax
from jax.sharding import PartitionSpec as P

ITERS = 3
DIAG_SHIFT = 0.05
VISCOSITY = 0.5
GRAVITY = 0.1
GRADIENT_GAIN = 32.0
AXES = (("gx", 1), ("gy", 2), ("gz", 3))


def with_halo(cells, sides, width):
    for axis, dim in sides:
        count = lax.axis_size(axis)
        ends = count - 1
        head = lax.slice_in_dim(cells, 0, width, axis=dim)
        tail = lax.slice_in_dim(cells, cells.shape[dim] - width, cells.shape[dim], axis=dim)
        cells = jnp.concatenate(
            [
                lax.ppermute(tail, axis, [(i, (i + 1) % count) for i in range(ends)]),
                cells,
                lax.ppermute(head, axis, [((i + 1) % count, i) for i in range(ends)]),
            ],
            axis=dim,
        )
    return cells


def neighbours(rim):
    comps, size_x, size_y, size_z, width = rim.shape
    blocks = []
    for ax in range(size_x - 2):
        for ay in range(size_y - 2):
            for az in range(size_z - 2):
                window = rim[:, ax : ax + 3, ay : ay + 3, az : az + 3, :]
                blocks.append(window.reshape(comps, 27 * width))
    return jnp.stack(blocks, axis=1)


def flat(cells):
    return cells.reshape(cells.shape[0], -1, cells.shape[4])


def wsum(weight, near):
    return jnp.sum(weight[None] * near[:, :, None, :], axis=-1)


def tile_corners(block_shape):
    _, size_x, size_y, size_z, _ = block_shape
    base = (
        lax.axis_index("gx") * size_x,
        lax.axis_index("gy") * size_y,
        lax.axis_index("gz") * size_z,
    )
    corners = []
    for ax in range(size_x):
        for ay in range(size_y):
            for az in range(size_z):
                corners.append(jnp.stack([base[0] + ax, base[1] + ay, base[2] + az]))
    return jnp.stack(corners, axis=1).astype(jnp.float32)


def on_device(positions, velocity, counts):
    block_shape = positions.shape
    width = positions.shape[4]
    slot_ids = jnp.arange(width, dtype=jnp.int32)
    valid_mask = (slot_ids[None, None, None, :] < counts[:, :, :, None]).astype(jnp.float32)[None]
    packed = jnp.concatenate([positions, valid_mask, velocity], axis=0)
    near_all = neighbours(with_halo(packed, AXES, 1))
    near_x = near_all[0:3]
    near_valid = near_all[3]
    near_v = near_all[4:7]
    own_x = flat(positions)
    own_valid = flat(valid_mask)[0]
    own_v = flat(velocity)
    offset = own_x[:, :, :, None] - near_x[:, :, None, :]
    distance = offset[0] * offset[0] + offset[1] * offset[1] + offset[2] * offset[2]
    closeness = jnp.maximum(1.0 - distance, 0.0)
    weight = closeness * closeness * own_valid[:, :, None] * near_valid[:, None, :]
    corner = tile_corners(block_shape)[:, :, None]
    local_own = own_x - corner
    local_near = near_x - corner
    row = jnp.sum(weight, axis=-1)[None]
    sums = wsum(weight, jnp.concatenate([near_v, local_near], axis=0))
    near_sums = sums[0:3]
    lever = local_own * row - sums[3:6]
    gravity_pull = jnp.array([0.0, 0.0, -GRAVITY], jnp.float32).reshape(3, 1, 1)
    predicted = own_valid[None] * (
        own_v + VISCOSITY / width * (near_sums - row * own_v) + gravity_pull
    )
    diagonal = DIAG_SHIFT + row / width

    def shaped(values):
        return values.reshape(values.shape[0], *block_shape[1:])

    near_pred = neighbours(with_halo(shaped(predicted), AXES, 1))
    dotted = jnp.sum(near_pred * local_near, axis=0, keepdims=True)
    psums = wsum(weight, jnp.concatenate([near_pred, dotted], axis=0))
    flux = jnp.sum(local_own * psums[0:3], axis=0, keepdims=True) - psums[3:4]
    source = -(GRADIENT_GAIN / width) * (jnp.sum(predicted * lever, axis=0, keepdims=True) - flux)

    def operate(field):
        near_field = neighbours(with_halo(shaped(field), AXES, 1))
        return (near_field, diagonal * field - wsum(weight, near_field) / width)

    def paired_sums(residual, precond, applied):
        pair = jnp.stack([jnp.sum(residual * precond), jnp.sum(precond * applied)])
        total = lax.psum(pair, ("gx", "gy", "gz"))
        return (total[0], total[1])

    pressure = jnp.zeros_like(source)
    residual = source
    precond = residual / diagonal
    near_dir, applied = operate(precond)
    norm_now, curvature_sum = paired_sums(residual, precond, applied)
    step_size = norm_now / curvature_sum
    direction = precond
    along = applied
    near_pressure = jnp.zeros_like(near_dir)
    for iteration in range(ITERS):
        pressure = pressure + step_size * direction
        near_pressure = near_pressure + step_size * near_dir
        residual = residual - step_size * along
        if iteration + 1 < ITERS:
            precond = residual / diagonal
            near_fresh, applied = operate(precond)
            norm_next, curvature_sum = paired_sums(residual, precond, applied)
            blend = norm_next / norm_now
            step_size = norm_next / (curvature_sum - blend * norm_next / step_size)
            direction = precond + blend * direction
            near_dir = near_fresh + blend * near_dir
            along = applied + blend * along
            norm_now = norm_next
    grads = wsum(weight, jnp.concatenate([near_pressure, near_pressure * local_near], axis=0))
    moments = local_own * grads[0:1] - grads[1:4]
    velocity_new = predicted - GRADIENT_GAIN / width * (pressure * lever - moments)
    return (shaped(velocity_new), shaped(pressure)[0])


def solution(mesh):
    in_specs = (
        P(None, "gx", "gy", "gz", None),
        P(None, "gx", "gy", "gz", None),
        P("gx", "gy", "gz"),
    )
    out_specs = (P(None, "gx", "gy", "gz", None), P("gx", "gy", "gz", None))
    return jax.shard_map(
        on_device, mesh=mesh, in_specs=in_specs, out_specs=out_specs, check_vma=False
    )
```

profile of v0, /device:TPU:0, one launch (start us, length us, event | category | flops | bytes accessed | tf_op | source)
XLA Modules:
  0.0 319.3 jit_solution(7614055411883678423)
XLA Ops:
  4.0 5.6 %collective-permute-start = (f32[7,1,1,2,128]{4,0,3,2,1:T(8,128)S(1)}, f32[7,1,1,2,128]{4,0,3,2,1:T(8,128)S(1)}, u32[]{:S(2)}, u32[]{:S(2)}) collective-permute-start(f32[7,1,1,2,128]{4,0,3,2,1:T(8,128)S(1)} %pad_maximum_fusion.19), channel_id=1, source_target_pairs={{0,8},{8,16},{16,24},{1,9},{9,17},{17,25},{2,10},{10,18},{18,26},{... | collective-permute-start | bytes 21512 | tf_op jit(solution)/shard_map/ppermute | solution.py:22
  12.3 4.5 %collective-permute-start.2 = (f32[7,3,1,2,128]{4,0,3,2,1:T(8,128)S(1)}, f32[7,3,1,2,128]{4,0,3,2,1:T(8,128)S(1)}, u32[]{:S(2)}, u32[]{:S(2)}) collective-permute-start(f32[7,3,1,2,128]{4,0,3,2,1:T(8,128)S(1)} %pad_maximum_fusion.11), channel_id=1, source_target_pairs={{0,4},{1,5},{2,6},{3,7},{8,12},{9,13},{10,14},{11,15},{16,20},{17,... | collective-permute-start | bytes 64520 | tf_op jit(solution)/shard_map/ppermute | solution.py:22
  21.0 3.9 %collective-permute-done.5 = f32[7,3,3,1,128]{4,0,3,2,1:T(8,128)S(1)} collective-permute-done((f32[7,3,3,1,128]{4,0,3,2,1:T(8,128)S(1)}, f32[7,3,3,1,128]{4,0,3,2,1:T(8,128)S(1)}, u32[]{:S(2)}, u32[]{:S(2)}) %collective-permute-start.5) | collective-permute-done | bytes 32288 | tf_op jit(solution)/shard_map/ppermute | solution.py:24
  29.3 1.7 copy-done
  31.0 1.8 multiply_reduce_fusion
  34.2 4.8 %collective-permute-start.6 = (f32[3,1,1,2,128]{4,3,0,2,1:T(2,128)S(1)}, f32[3,1,1,2,128]{4,3,0,2,1:T(2,128)S(1)}, u32[]{:S(2)}, u32[]{:S(2)}) collective-permute-start(f32[3,1,1,2,128]{4,3,0,2,1:T(2,128)S(1)} %bitcast.144), channel_id=1, source_target_pairs={{0,8},{8,16},{16,24},{1,9},{9,17},{17,25},{2,10},{10,18},{18,26},{... | collective-permute-start | bytes 9224 | tf_op jit(solution)/shard_map/ppermute | solution.py:22
  41.7 4.5 %collective-permute-start.8 = (f32[3,3,1,2,128]{4,3,0,2,1:T(2,128)S(1)}, f32[3,3,1,2,128]{4,3,0,2,1:T(2,128)S(1)}, u32[]{:S(2)}, u32[]{:S(2)}) collective-permute-start(f32[3,3,1,2,128]{4,3,0,2,1:T(2,128)S(1)} %pad_maximum_fusion.15), channel_id=1, source_target_pairs={{0,4},{1,5},{2,6},{3,7},{8,12},{9,13},{10,14},{11,15},{16,20},{17,... | collective-permute-start | bytes 27656 | tf_op jit(solution)/shard_map/ppermute | solution.py:22
  49.5 3.8 %collective-permute-start.10 = (f32[3,3,3,1,128]{4,3,0,2,1:T(1,128)}, f32[3,3,3,1,128]{4,3,0,2,1:T(1,128)}, u32[]{:S(2)}, u32[]{:S(2)}) collective-permute-start(f32[3,3,3,1,128]{4,3,0,2,1:T(1,128)} %get-tuple-element.28), channel_id=1, source_target_pairs={{0,1},{1,2},{2,3},{4,5},{5,6},{6,7},{8,9},{9,10},{10,11},{12,13},{... | collective-permute-start | bytes 41480 | tf_op jit(solution)/shard_map/ppermute | solution.py:22
  66.1 3.3 %multiply_reduce_fusion.2 = f32[4,2,128]{2,1,0:T(2,128)S(1)} fusion(f32[4,2,3456]{2,1,0:T(2,128)S(1)} %copy.34, f32[2,128,3456]{2,1,0:T(8,128)} %copy-done), kind=kLoop, calls=%fused_computation.2 | loop fusion | flops 7076864 | bytes 3653632 | tf_op jit(solution)/shard_map/reduce_sum | solution.py:47
  71.4 4.6 %collective-permute-start.12 = (f32[1,1,1,2,128]{4,3,2,1,0:T(2,128)S(1)}, f32[1,1,1,2,128]{4,3,2,1,0:T(2,128)S(1)}, u32[]{:S(2)}, u32[]{:S(2)}) collective-permute-start(f32[1,1,1,2,128]{4,3,2,1,0:T(2,128)S(1)} %bitcast.160), channel_id=1, source_target_pairs={{0,8},{8,16},{16,24},{1,9},{9,17},{17,25},{2,10},{10,18},{18,26},{... | collective-permute-start | bytes 3080 | tf_op jit(solution)/shard_map/ppermute | solution.py:22
  78.6 4.5 %collective-permute-start.14 = (f32[1,3,1,2,128]{4,3,2,1,0:T(2,128)S(1)}, f32[1,3,1,2,128]{4,3,2,1,0:T(2,128)S(1)}, u32[]{:S(2)}, u32[]{:S(2)}) collective-permute-start(f32[1,3,1,2,128]{4,3,2,1,0:T(2,128)S(1)} %pad_maximum_fusion.20), channel_id=1, source_target_pairs={{0,4},{1,5},{2,6},{3,7},{8,12},{9,13},{10,14},{11,15},{16,20},{17,... | collective-permute-start | bytes 9224 | tf_op jit(solution)/shard_map/ppermute | solution.py:22
  87.3 5.3 %collective-permute-done.17 = f32[1,3,3,1,128]{4,3,2,1,0:T(1,128)S(1)} collective-permute-done((f32[1,3,3,1,128]{4,3,2,1,0:T(1,128)S(1)}, f32[1,3,3,1,128]{4,3,2,1,0:T(1,128)S(1)}, u32[]{:S(2)}, u32[]{:S(2)}) %collective-permute-start.17) | collective-permute-done | bytes 4640 | tf_op jit(solution)/shard_map/ppermute | solution.py:24
  98.8 1.8 pad_maximum_fusion.23
  100.6 43.4 %psum.21 = f32[2]{0:T(128)} all-reduce(f32[2]{0:T(128)} %pad_maximum_fusion.23), channel_id=1, replica_groups=mesh['gx'=4,'gy'=2,'gz'=4] {'gx','gy','gz'}, use_global_device_ids=true, to_apply=%region_9.0 | all-reduce | flops 2 | bytes 16 | tf_op jit(solution)/shard_map/psum | solution.py:110
  148.7 4.5 %collective-permute-start.18 = (f32[1,1,1,2,128]{4,3,2,1,0:T(2,128)S(1)}, f32[1,1,1,2,128]{4,3,2,1,0:T(2,128)S(1)}, u32[]{:S(2)}, u32[]{:S(2)}) collective-permute-start(f32[1,1,1,2,128]{4,3,2,1,0:T(2,128)S(1)} %bitcast.149), channel_id=1, source_target_pairs={{0,8},{8,16},{16,24},{1,9},{9,17},{17,25},{2,10},{10,18},{18,26},{... | collective-permute-start | bytes 3080 | tf_op jit(solution)/shard_map/ppermute | solution.py:22
  155.9 4.5 %collective-permute-start.20 = (f32[1,3,1,2,128]{4,3,2,1,0:T(2,128)S(1)}, f32[1,3,1,2,128]{4,3,2,1,0:T(2,128)S(1)}, u32[]{:S(2)}, u32[]{:S(2)}) collective-permute-start(f32[1,3,1,2,128]{4,3,2,1,0:T(2,128)S(1)} %pad_maximum_fusion.21), channel_id=1, source_target_pairs={{0,4},{1,5},{2,6},{3,7},{8,12},{9,13},{10,14},{11,15},{16,20},{17,... | collective-permute-start | bytes 9224 | tf_op jit(solution)/shard_map/ppermute | solution.py:22
  164.4 4.3 %collective-permute-done.23 = f32[1,3,3,1,128]{4,3,2,1,0:T(1,128)S(1)} collective-permute-done((f32[1,3,3,1,128]{4,3,2,1,0:T(1,128)S(1)}, f32[1,3,3,1,128]{4,3,2,1,0:T(1,128)S(1)}, u32[]{:S(2)}, u32[]{:S(2)}) %collective-permute-start.23) | collective-permute-done | bytes 4640 | tf_op jit(solution)/shard_map/ppermute | solution.py:24
  175.5 1.8 pad_maximum_fusion.24
  177.4 43.4 %psum.22 = f32[2]{0:T(128)} all-reduce(f32[2]{0:T(128)} %pad_maximum_fusion.24), channel_id=1, replica_groups=mesh['gx'=4,'gy'=2,'gz'=4] {'gx','gy','gz'}, use_global_device_ids=true, to_apply=%region_13.0 | all-reduce | flops 2 | bytes 16 | tf_op jit(solution)/shard_map/psum | solution.py:110
  229.1 4.5 %collective-permute-start.24 = (f32[1,1,1,2,128]{4,3,2,1,0:T(2,128)S(1)}, f32[1,1,1,2,128]{4,3,2,1,0:T(2,128)S(1)}, u32[]{:S(2)}, u32[]{:S(2)}) collective-permute-start(f32[1,1,1,2,128]{4,3,2,1,0:T(2,128)S(1)} %bitcast.155), channel_id=1, source_target_pairs={{0,8},{8,16},{16,24},{1,9},{9,17},{17,25},{2,10},{10,18},{18,26},{... | collective-permute-start | bytes 3080 | tf_op jit(solution)/shard_map/ppermute | solution.py:22
  236.3 4.5 %collective-permute-start.26 = (f32[1,3,1,2,128]{4,3,2,1,0:T(2,128)S(1)}, f32[1,3,1,2,128]{4,3,2,1,0:T(2,128)S(1)}, u32[]{:S(2)}, u32[]{:S(2)}) collective-permute-start(f32[1,3,1,2,128]{4,3,2,1,0:T(2,128)S(1)} %pad_maximum_fusion.22), channel_id=1, source_target_pairs={{0,4},{1,5},{2,6},{3,7},{8,12},{9,13},{10,14},{11,15},{16,20},{17,... | collective-permute-start | bytes 9224 | tf_op jit(solution)/shard_map/ppermute | solution.py:22
  242.7 1.9 collective-permute-start.28
  262.5 45.0 %psum.23 = f32[2]{0:T(128)S(1)} all-reduce(f32[2]{0:T(128)S(1)} %pad_maximum_fusion.25), channel_id=1, replica_groups=mesh['gx'=4,'gy'=2,'gz'=4] {'gx','gy','gz'}, use_global_device_ids=true, to_apply=%region_17.0 | all-reduce | flops 2 | bytes 16 | tf_op jit(solution)/shard_map/psum | solution.py:110
  315.3 3.3 %multiply_reduce_fusion.1 = f32[4,2,128]{2,1,0:T(2,128)S(1)} fusion(f32[4,2,3456]{2,1,0:T(2,128)S(1)} %copy.41, f32[2,128,3456]{2,1,0:T(8,128)} %copy-done), kind=kLoop, calls=%fused_computation.1 | loop fusion | flops 7076864 | bytes 3653632 | tf_op jit(solution)/shard_map/reduce_sum | solution.py:47
  (206 shorter events, 96.7 us)
Async XLA Ops:
  2.7 7.6 %collective-permute-start.1 = (f32[7,1,1,2,128]{4,0,3,2,1:T(8,128)S(1)}, f32[7,1,1,2,128]{4,0,3,2,1:T(8,128)S(1)}, u32[]{:S(2)}, u32[]{:S(2)}) collective-permute-start(f32[7,1,1,2,128]{4,0,3,2,1:T(8,128)S(1)} %pad_maximum_fusion.19), channel_id=1, source_target_pairs={{8,0},{16,8},{24,16},{9,1},{17,9},{25,17},{10,2},{18,10},{26,18},{... | collective-permute-start | bytes 21512 | tf_op jit(solution)/shard_map/ppermute | solution.py:24
  4.0 6.9 %collective-permute-start = (f32[7,1,1,2,128]{4,0,3,2,1:T(8,128)S(1)}, f32[7,1,1,2,128]{4,0,3,2,1:T(8,128)S(1)}, u32[]{:S(2)}, u32[]{:S(2)}) collective-permute-start(f32[7,1,1,2,128]{4,0,3,2,1:T(8,128)S(1)} %pad_maximum_fusion.19), channel_id=1, source_target_pairs={{0,8},{8,16},{16,24},{1,9},{9,17},{17,25},{2,10},{10,18},{18,26},{... | collective-permute-start | bytes 21512 | tf_op jit(solution)/shard_map/ppermute | solution.py:22
  11.0 5.9 %collective-permute-start.3 = (f32[7,3,1,2,128]{4,0,3,2,1:T(8,128)S(1)}, f32[7,3,1,2,128]{4,0,3,2,1:T(8,128)S(1)}, u32[]{:S(2)}, u32[]{:S(2)}) collective-permute-start(f32[7,3,1,2,128]{4,0,3,2,1:T(8,128)S(1)} %pad_maximum_fusion.11), channel_id=1, source_target_pairs={{4,0},{5,1},{6,2},{7,3},{12,8},{13,9},{14,10},{15,11},{20,16},{21,... | collective-permute-start | bytes 64520 | tf_op jit(solution)/shard_map/ppermute | solution.py:24
  12.3 6.1 %collective-permute-start.2 = (f32[7,3,1,2,128]{4,0,3,2,1:T(8,128)S(1)}, f32[7,3,1,2,128]{4,0,3,2,1:T(8,128)S(1)}, u32[]{:S(2)}, u32[]{:S(2)}) collective-permute-start(f32[7,3,1,2,128]{4,0,3,2,1:T(8,128)S(1)} %pad_maximum_fusion.11), channel_id=1, source_target_pairs={{0,4},{1,5},{2,6},{3,7},{8,12},{9,13},{10,14},{11,15},{16,20},{17,... | collective-permute-start | bytes 64520 | tf_op jit(solution)/shard_map/ppermute | solution.py:22
  32.9 6.1 %collective-permute-start.7 = (f32[3,1,1,2,128]{4,3,0,2,1:T(2,128)S(1)}, f32[3,1,1,2,128]{4,3,0,2,1:T(2,128)S(1)}, u32[]{:S(2)}, u32[]{:S(2)}) collective-permute-start(f32[3,1,1,2,128]{4,3,0,2,1:T(2,128)S(1)} %bitcast.143), channel_id=1, source_target_pairs={{8,0},{16,8},{24,16},{9,1},{17,9},{25,17},{10,2},{18,10},{26,18},{... | collective-permute-start | bytes 9224 | tf_op jit(solution)/shard_map/ppermute | solution.py:24
  34.2 6.1 %collective-permute-start.6 = (f32[3,1,1,2,128]{4,3,0,2,1:T(2,128)S(1)}, f32[3,1,1,2,128]{4,3,0,2,1:T(2,128)S(1)}, u32[]{:S(2)}, u32[]{:S(2)}) collective-permute-start(f32[3,1,1,2,128]{4,3,0,2,1:T(2,128)S(1)} %bitcast.144), channel_id=1, source_target_pairs={{0,8},{8,16},{16,24},{1,9},{9,17},{17,25},{2,10},{10,18},{18,26},{... | collective-permute-start | bytes 9224 | tf_op jit(solution)/shard_map/ppermute | solution.py:22
  40.4 5.9 %collective-permute-start.9 = (f32[3,3,1,2,128]{4,3,0,2,1:T(2,128)S(1)}, f32[3,3,1,2,128]{4,3,0,2,1:T(2,128)S(1)}, u32[]{:S(2)}, u32[]{:S(2)}) collective-permute-start(f32[3,3,1,2,128]{4,3,0,2,1:T(2,128)S(1)} %pad_maximum_fusion.15), channel_id=1, source_target_pairs={{4,0},{5,1},{6,2},{7,3},{12,8},{13,9},{14,10},{15,11},{20,16},{21,... | collective-permute-start | bytes 27656 | tf_op jit(solution)/shard_map/ppermute | solution.py:24
  41.7 5.9 %collective-permute-start.8 = (f32[3,3,1,2,128]{4,3,0,2,1:T(2,128)S(1)}, f32[3,3,1,2,128]{4,3,0,2,1:T(2,128)S(1)}, u32[]{:S(2)}, u32[]{:S(2)}) collective-permute-start(f32[3,3,1,2,128]{4,3,0,2,1:T(2,128)S(1)} %pad_maximum_fusion.15), channel_id=1, source_target_pairs={{0,4},{1,5},{2,6},{3,7},{8,12},{9,13},{10,14},{11,15},{16,20},{17,... | collective-permute-start | bytes 27656 | tf_op jit(solution)/shard_map/ppermute | solution.py:22
  48.2 6.5 %collective-permute-start.11 = (f32[3,3,3,1,128]{4,3,0,2,1:T(1,128)}, f32[3,3,3,1,128]{4,3,0,2,1:T(1,128)}, u32[]{:S(2)}, u32[]{:S(2)}) collective-permute-start(f32[3,3,3,1,128]{4,3,0,2,1:T(1,128)} %get-tuple-element.27), channel_id=1, source_target_pairs={{1,0},{2,1},{3,2},{5,4},{6,5},{7,6},{9,8},{10,9},{11,10},{13,12},{... | collective-permute-start | bytes 41480 | tf_op jit(solution)/shard_map/ppermute | solution.py:24
  70.1 5.9 %collective-permute-start.13 = (f32[1,1,1,2,128]{4,3,2,1,0:T(2,128)S(1)}, f32[1,1,1,2,128]{4,3,2,1,0:T(2,128)S(1)}, u32[]{:S(2)}, u32[]{:S(2)}) collective-permute-start(f32[1,1,1,2,128]{4,3,2,1,0:T(2,128)S(1)} %bitcast.159), channel_id=1, source_target_pairs={{8,0},{16,8},{24,16},{9,1},{17,9},{25,17},{10,2},{18,10},{26,18},{... | collective-permute-start | bytes 3080 | tf_op jit(solution)/shard_map/ppermute | solution.py:24
  71.4 5.9 %collective-permute-start.12 = (f32[1,1,1,2,128]{4,3,2,1,0:T(2,128)S(1)}, f32[1,1,1,2,128]{4,3,2,1,0:T(2,128)S(1)}, u32[]{:S(2)}, u32[]{:S(2)}) collective-permute-start(f32[1,1,1,2,128]{4,3,2,1,0:T(2,128)S(1)} %bitcast.160), channel_id=1, source_target_pairs={{0,8},{8,16},{16,24},{1,9},{9,17},{17,25},{2,10},{10,18},{18,26},{... | collective-permute-start | bytes 3080 | tf_op jit(solution)/shard_map/ppermute | solution.py:22
  77.3 5.8 %collective-permute-start.15 = (f32[1,3,1,2,128]{4,3,2,1,0:T(2,128)S(1)}, f32[1,3,1,2,128]{4,3,2,1,0:T(2,128)S(1)}, u32[]{:S(2)}, u32[]{:S(2)}) collective-permute-start(f32[1,3,1,2,128]{4,3,2,1,0:T(2,128)S(1)} %pad_maximum_fusion.20), channel_id=1, source_target_pairs={{4,0},{5,1},{6,2},{7,3},{12,8},{13,9},{14,10},{15,11},{20,16},{21,... | collective-permute-start | bytes 9224 | tf_op jit(solution)/shard_map/ppermute | solution.py:24
  78.6 5.9 %collective-permute-start.14 = (f32[1,3,1,2,128]{4,3,2,1,0:T(2,128)S(1)}, f32[1,3,1,2,128]{4,3,2,1,0:T(2,128)S(1)}, u32[]{:S(2)}, u32[]{:S(2)}) collective-permute-start(f32[1,3,1,2,128]{4,3,2,1,0:T(2,128)S(1)} %pad_maximum_fusion.20), channel_id=1, source_target_pairs={{0,4},{1,5},{2,6},{3,7},{8,12},{9,13},{10,14},{11,15},{16,20},{17,... | collective-permute-start | bytes 9224 | tf_op jit(solution)/shard_map/ppermute | solution.py:22
  86.0 6.6 %collective-permute-start.17 = (f32[1,3,3,1,128]{4,3,2,1,0:T(1,128)S(1)}, f32[1,3,3,1,128]{4,3,2,1,0:T(1,128)S(1)}, u32[]{:S(2)}, u32[]{:S(2)}) collective-permute-start(f32[1,3,3,1,128]{4,3,2,1,0:T(1,128)S(1)} %get-tuple-element.40), channel_id=1, source_target_pairs={{1,0},{2,1},{3,2},{5,4},{6,5},{7,6},{9,8},{10,9},{11,10},{13,12},{... | collective-permute-start | bytes 13832 | tf_op jit(solution)/shard_map/ppermute | solution.py:24
  147.5 5.8 %collective-permute-start.19 = (f32[1,1,1,2,128]{4,3,2,1,0:T(2,128)S(1)}, f32[1,1,1,2,128]{4,3,2,1,0:T(2,128)S(1)}, u32[]{:S(2)}, u32[]{:S(2)}) collective-permute-start(f32[1,1,1,2,128]{4,3,2,1,0:T(2,128)S(1)} %bitcast.148), channel_id=1, source_target_pairs={{8,0},{16,8},{24,16},{9,1},{17,9},{25,17},{10,2},{18,10},{26,18},{... | collective-permute-start | bytes 3080 | tf_op jit(solution)/shard_map/ppermute | solution.py:24
  148.7 5.8 %collective-permute-start.18 = (f32[1,1,1,2,128]{4,3,2,1,0:T(2,128)S(1)}, f32[1,1,1,2,128]{4,3,2,1,0:T(2,128)S(1)}, u32[]{:S(2)}, u32[]{:S(2)}) collective-permute-start(f32[1,1,1,2,128]{4,3,2,1,0:T(2,128)S(1)} %bitcast.149), channel_id=1, source_target_pairs={{0,8},{8,16},{16,24},{1,9},{9,17},{17,25},{2,10},{10,18},{18,26},{... | collective-permute-start | bytes 3080 | tf_op jit(solution)/shard_map/ppermute | solution.py:22
  154.6 5.8 %collective-permute-start.21 = (f32[1,3,1,2,128]{4,3,2,1,0:T(2,128)S(1)}, f32[1,3,1,2,128]{4,3,2,1,0:T(2,128)S(1)}, u32[]{:S(2)}, u32[]{:S(2)}) collective-permute-start(f32[1,3,1,2,128]{4,3,2,1,0:T(2,128)S(1)} %pad_maximum_fusion.21), channel_id=1, source_target_pairs={{4,0},{5,1},{6,2},{7,3},{12,8},{13,9},{14,10},{15,11},{20,16},{21,... | collective-permute-start | bytes 9224 | tf_op jit(solution)/shard_map/ppermute | solution.py:24
  155.9 5.9 %collective-permute-start.20 = (f32[1,3,1,2,128]{4,3,2,1,0:T(2,128)S(1)}, f32[1,3,1,2,128]{4,3,2,1,0:T(2,128)S(1)}, u32[]{:S(2)}, u32[]{:S(2)}) collective-permute-start(f32[1,3,1,2,128]{4,3,2,1,0:T(2,128)S(1)} %pad_maximum_fusion.21), channel_id=1, source_target_pairs={{0,4},{1,5},{2,6},{3,7},{8,12},{9,13},{10,14},{11,15},{16,20},{17,... | collective-permute-start | bytes 9224 | tf_op jit(solution)/shard_map/ppermute | solution.py:22
  227.9 5.8 %collective-permute-start.25 = (f32[1,1,1,2,128]{4,3,2,1,0:T(2,128)S(1)}, f32[1,1,1,2,128]{4,3,2,1,0:T(2,128)S(1)}, u32[]{:S(2)}, u32[]{:S(2)}) collective-permute-start(f32[1,1,1,2,128]{4,3,2,1,0:T(2,128)S(1)} %bitcast.154), channel_id=1, source_target_pairs={{8,0},{16,8},{24,16},{9,1},{17,9},{25,17},{10,2},{18,10},{26,18},{... | collective-permute-start | bytes 3080 | tf_op jit(solution)/shard_map/ppermute | solution.py:24
  229.1 5.8 %collective-permute-start.24 = (f32[1,1,1,2,128]{4,3,2,1,0:T(2,128)S(1)}, f32[1,1,1,2,128]{4,3,2,1,0:T(2,128)S(1)}, u32[]{:S(2)}, u32[]{:S(2)}) collective-permute-start(f32[1,1,1,2,128]{4,3,2,1,0:T(2,128)S(1)} %bitcast.155), channel_id=1, source_target_pairs={{0,8},{8,16},{16,24},{1,9},{9,17},{17,25},{2,10},{10,18},{18,26},{... | collective-permute-start | bytes 3080 | tf_op jit(solution)/shard_map/ppermute | solution.py:22
  235.0 5.8 %collective-permute-start.27 = (f32[1,3,1,2,128]{4,3,2,1,0:T(2,128)S(1)}, f32[1,3,1,2,128]{4,3,2,1,0:T(2,128)S(1)}, u32[]{:S(2)}, u32[]{:S(2)}) collective-permute-start(f32[1,3,1,2,128]{4,3,2,1,0:T(2,128)S(1)} %pad_maximum_fusion.22), channel_id=1, source_target_pairs={{4,0},{5,1},{6,2},{7,3},{12,8},{13,9},{14,10},{15,11},{20,16},{21,... | collective-permute-start | bytes 9224 | tf_op jit(solution)/shard_map/ppermute | solution.py:24
  236.3 5.9 %collective-permute-start.26 = (f32[1,3,1,2,128]{4,3,2,1,0:T(2,128)S(1)}, f32[1,3,1,2,128]{4,3,2,1,0:T(2,128)S(1)}, u32[]{:S(2)}, u32[]{:S(2)}) collective-permute-start(f32[1,3,1,2,128]{4,3,2,1,0:T(2,128)S(1)} %pad_maximum_fusion.22), channel_id=1, source_target_pairs={{0,4},{1,5},{2,6},{3,7},{8,12},{9,13},{10,14},{11,15},{16,20},{17,... | collective-permute-start | bytes 9224 | tf_op jit(solution)/shard_map/ppermute | solution.py:22
  242.7 8.7 %collective-permute-start.28 = (f32[1,3,3,1,128]{4,3,2,1,0:T(1,128)}, f32[1,3,3,1,128]{4,3,2,1,0:T(1,128)}, u32[]{:S(2)}, u32[]{:S(2)}) collective-permute-start(f32[1,3,3,1,128]{4,3,2,1,0:T(1,128)} %get-tuple-element.31), channel_id=1, source_target_pairs={{0,1},{1,2},{2,3},{4,5},{5,6},{6,7},{8,9},{9,10},{10,11},{12,13},{... | collective-permute-start | bytes 13832 | tf_op jit(solution)/shard_map/ppermute | solution.py:22
  244.6 6.8 %collective-permute-start.29 = (f32[1,3,3,1,128]{4,3,2,1,0:T(1,128)}, f32[1,3,3,1,128]{4,3,2,1,0:T(1,128)}, u32[]{:S(2)}, u32[]{:S(2)}) collective-permute-start(f32[1,3,3,1,128]{4,3,2,1,0:T(1,128)} %get-tuple-element.32), channel_id=1, source_target_pairs={{1,0},{2,1},{3,2},{5,4},{6,5},{7,6},{9,8},{10,9},{11,10},{13,12},{... | collective-permute-start | bytes 13832 | tf_op jit(solution)/shard_map/ppermute | solution.py:24
  (43 other events, 650.6 us)
where the time goes:
time: 322 us; the launch traced here: 319 us
  blocking collectives  132 us (41%)
  starting transfers between devices  76 us (24%)
  other arithmetic  41.9 us (13%)
  local copies, waits for them, and re-layouts  32.6 us (10%)
  waiting for transfers between devices  25.9 us (8%)
  between operations  11.2 us (3%)
    psum x3, blocking collectives, paired_sums(): total = lax.psum(pair, ('gx', 'gy', 'gz'))  132 us
    ppermute x15, starting transfers between devices, with_halo(): lax.ppermute(tail, axis, [(i, (i + 1) % count) for i in range(ends)])  56.6 us
    ppermute x15, starting transfers between devices, with_halo(): lax.ppermute(head, axis, [((i + 1) % count, i) for i in range(ends)])  19.5 us
    another operation x15, local copies, waits for them, and re-layouts, neighbours(): return jnp.stack(blocks, axis=1)  19.3 us
    ppermute x15, waiting for transfers between devices, with_halo(): lax.ppermute(head, axis, [((i + 1) % count, i) for i in range(ends)])  13.5 us
    reduce_sum x6, other arithmetic, wsum(): return jnp.sum(weight[None] * near[:, :, None, :], axis=-1)  12.6 us
    ppermute x15, waiting for transfers between devices, with_halo(): lax.ppermute(tail, axis, [(i, (i + 1) % count) for i in range(ends)])  12.3 us
  transfers between devices with their start and end apart: 30, of which 13 were waited for; matrix products, arithmetic and copies ran while one was open for 2% of the time, Pallas kernels for 0%

commit v1 on v0

--- a/solution.py
+++ b/solution.py
@@ -107,7 +107,7 @@
 
     def paired_sums(residual, precond, applied):
         pair = jnp.stack([jnp.sum(residual * precond), jnp.sum(precond * applied)])
-        total = lax.psum(pair, ("gx", "gy", "gz"))
+        total = jnp.sum(lax.all_gather(pair, ("gx", "gy", "gz")), axis=0)
         return (total[0], total[1])
 
     pressure = jnp.zeros_like(source)

time: 322 us -> 333 us (1.034)
  other arithmetic: 41.9 us -> 46.9 us
  local copies, waits for them, and re-layouts: 32.6 us -> 37.4 us
    psum x3 -> x0, blocking collectives: 132 us -> none  [paired_sums(): total = lax.psum(pair, ('gx', 'gy', 'gz'))]
    unnamed x0 -> x3, blocking collectives: none -> 132 us
    unnamed x1 -> x4, other arithmetic: 0.66 us -> 7.33 us
    another operation x3 -> x0, other arithmetic: 4.92 us -> none  [paired_sums(): pair = jnp.stack([jnp.sum(residual * precond), jnp.sum(precond * applied)])]
where the time goes in v1:
time: 333 us; the launch traced here: 329 us
  blocking collectives  132 us (40%)
  starting transfers between devices  76.6 us (23%)
  other arithmetic  46.9 us (14%)
  local copies, waits for them, and re-layouts  37.4 us (11%)
  waiting for transfers between devices  25.6 us (8%)
  between operations  11.2 us (3%)
    unnamed x3, blocking collectives  132 us
    ppermute x15, starting transfers between devices, with_halo(): lax.ppermute(tail, axis, [(i, (i + 1) % count) for i in range(ends)])  57.2 us
    another operation x15, local copies, waits for them, and re-layouts, neighbours(): return jnp.stack(blocks, axis=1)  19.9 us
    ppermute x15, starting transfers between devices, with_halo(): lax.ppermute(head, axis, [((i + 1) % count, i) for i in range(ends)])  19.4 us
    ppermute x15, waiting for transfers between devices, with_halo(): lax.ppermute(head, axis, [((i + 1) % count, i) for i in range(ends)])  13.3 us
    reduce_sum x6, other arithmetic, wsum(): return jnp.sum(weight[None] * near[:, :, None, :], axis=-1)  12.5 us
    ppermute x15, waiting for transfers between devices, with_halo(): lax.ppermute(tail, axis, [(i, (i + 1) % count) for i in range(ends)])  12.3 us
    unnamed x4, other arithmetic  7.33 us
  transfers between devices with their start and end apart: 30, of which 13 were waited for; matrix products, arithmetic and copies ran while one was open for 2% of the time, Pallas kernels for 0%

profile of v1, /device:TPU:0, one launch (start us, length us, event | category | flops | bytes accessed | tf_op | source)
XLA Modules:
  0.0 329.4 jit_solution(9682376368374518692)
XLA Ops:
  4.0 5.6 %collective-permute-start = (f32[7,1,1,2,128]{4,0,3,2,1:T(8,128)S(1)}, f32[7,1,1,2,128]{4,0,3,2,1:T(8,128)S(1)}, u32[]{:S(2)}, u32[]{:S(2)}) collective-permute-start(f32[7,1,1,2,128]{4,0,3,2,1:T(8,128)S(1)} %pad_maximum_fusion.19), channel_id=1, source_target_pairs={{0,8},{8,16},{16,24},{1,9},{9,17},{17,25},{2,10},{10,18},{18,26},{... | collective-permute-start | bytes 21512 | tf_op jit(solution)/shard_map/ppermute | solution.py:22
  12.3 4.5 %collective-permute-start.2 = (f32[7,3,1,2,128]{4,0,3,2,1:T(8,128)S(1)}, f32[7,3,1,2,128]{4,0,3,2,1:T(8,128)S(1)}, u32[]{:S(2)}, u32[]{:S(2)}) collective-permute-start(f32[7,3,1,2,128]{4,0,3,2,1:T(8,128)S(1)} %pad_maximum_fusion.11), channel_id=1, source_target_pairs={{0,4},{1,5},{2,6},{3,7},{8,12},{9,13},{10,14},{11,15},{16,20},{17,... | collective-permute-start | bytes 64520 | tf_op jit(solution)/shard_map/ppermute | solution.py:22
  21.0 3.9 %collective-permute-done.5 = f32[7,3,3,1,128]{4,0,3,2,1:T(8,128)S(1)} collective-permute-done((f32[7,3,3,1,128]{4,0,3,2,1:T(8,128)S(1)}, f32[7,3,3,1,128]{4,0,3,2,1:T(8,128)S(1)}, u32[]{:S(2)}, u32[]{:S(2)}) %collective-permute-start.5) | collective-permute-done | bytes 32288 | tf_op jit(solution)/shard_map/ppermute | solution.py:24
  30.7 1.8 multiply_reduce_fusion
  33.9 4.8 %collective-permute-start.6 = (f32[3,1,1,2,128]{4,3,0,2,1:T(2,128)S(1)}, f32[3,1,1,2,128]{4,3,0,2,1:T(2,128)S(1)}, u32[]{:S(2)}, u32[]{:S(2)}) collective-permute-start(f32[3,1,1,2,128]{4,3,0,2,1:T(2,128)S(1)} %bitcast.144), channel_id=1, source_target_pairs={{0,8},{8,16},{16,24},{1,9},{9,17},{17,25},{2,10},{10,18},{18,26},{... | collective-permute-start | bytes 9224 | tf_op jit(solution)/shard_map/ppermute | solution.py:22
  41.3 4.5 %collective-permute-start.8 = (f32[3,3,1,2,128]{4,3,0,2,1:T(2,128)S(1)}, f32[3,3,1,2,128]{4,3,0,2,1:T(2,128)S(1)}, u32[]{:S(2)}, u32[]{:S(2)}) collective-permute-start(f32[3,3,1,2,128]{4,3,0,2,1:T(2,128)S(1)} %pad_maximum_fusion.15), channel_id=1, source_target_pairs={{0,4},{1,5},{2,6},{3,7},{8,12},{9,13},{10,14},{11,15},{16,20},{17,... | collective-permute-start | bytes 27656 | tf_op jit(solution)/shard_map/ppermute | solution.py:22
  49.2 3.8 %collective-permute-start.10 = (f32[3,3,3,1,128]{4,3,0,2,1:T(1,128)}, f32[3,3,3,1,128]{4,3,0,2,1:T(1,128)}, u32[]{:S(2)}, u32[]{:S(2)}) collective-permute-start(f32[3,3,3,1,128]{4,3,0,2,1:T(1,128)} %get-tuple-element.28), channel_id=1, source_target_pairs={{0,1},{1,2},{2,3},{4,5},{5,6},{6,7},{8,9},{9,10},{10,11},{12,13},{... | collective-permute-start | bytes 41480 | tf_op jit(solution)/shard_map/ppermute | solution.py:22
  65.8 3.3 multiply_reduce_fusion.2
  71.0 4.6 %collective-permute-start.12 = (f32[1,1,1,2,128]{4,3,2,1,0:T(2,128)S(1)}, f32[1,1,1,2,128]{4,3,2,1,0:T(2,128)S(1)}, u32[]{:S(2)}, u32[]{:S(2)}) collective-permute-start(f32[1,1,1,2,128]{4,3,2,1,0:T(2,128)S(1)} %bitcast.160), channel_id=1, source_target_pairs={{0,8},{8,16},{16,24},{1,9},{9,17},{17,25},{2,10},{10,18},{18,26},{... | collective-permute-start | bytes 3080 | tf_op jit(solution)/shard_map/ppermute | solution.py:22
  78.3 4.5 %collective-permute-start.14 = (f32[1,3,1,2,128]{4,3,2,1,0:T(2,128)S(1)}, f32[1,3,1,2,128]{4,3,2,1,0:T(2,128)S(1)}, u32[]{:S(2)}, u32[]{:S(2)}) collective-permute-start(f32[1,3,1,2,128]{4,3,2,1,0:T(2,128)S(1)} %pad_maximum_fusion.20), channel_id=1, source_target_pairs={{0,4},{1,5},{2,6},{3,7},{8,12},{9,13},{10,14},{11,15},{16,20},{17,... | collective-permute-start | bytes 9224 | tf_op jit(solution)/shard_map/ppermute | solution.py:22
  84.7 2.1 collective-permute-start.16
  88.1 5.1 %collective-permute-done.17 = f32[1,3,3,1,128]{4,3,2,1,0:T(1,128)} collective-permute-done((f32[1,3,3,1,128]{4,3,2,1,0:T(1,128)}, f32[1,3,3,1,128]{4,3,2,1,0:T(1,128)}, u32[]{:S(2)}, u32[]{:S(2)}) %collective-permute-start.17) | collective-permute-done | bytes 4640 | tf_op jit(solution)/shard_map/ppermute | solution.py:24
  100.7 2.6 maximum_dynamic-update-slice_fusion
  103.3 43.4 %all-reduce = f32[64]{0:T(128)} all-reduce(f32[64]{0:T(128)} %maximum_dynamic-update-slice_fusion), channel_id=2, replica_groups=mesh['gx'=4,'gy'=2,'gz'=4] {'gx','gy','gz'}, use_global_device_ids=true, to_apply=%add | all-reduce | flops 64 | bytes 512
  153.9 4.5 %collective-permute-start.18 = (f32[1,1,1,2,128]{4,3,2,1,0:T(2,128)S(1)}, f32[1,1,1,2,128]{4,3,2,1,0:T(2,128)S(1)}, u32[]{:S(2)}, u32[]{:S(2)}) collective-permute-start(f32[1,1,1,2,128]{4,3,2,1,0:T(2,128)S(1)} %bitcast.149), channel_id=1, source_target_pairs={{0,8},{8,16},{16,24},{1,9},{9,17},{17,25},{2,10},{10,18},{18,26},{... | collective-permute-start | bytes 3080 | tf_op jit(solution)/shard_map/ppermute | solution.py:22
  161.0 4.5 %collective-permute-start.20 = (f32[1,3,1,2,128]{4,3,2,1,0:T(2,128)S(1)}, f32[1,3,1,2,128]{4,3,2,1,0:T(2,128)S(1)}, u32[]{:S(2)}, u32[]{:S(2)}) collective-permute-start(f32[1,3,1,2,128]{4,3,2,1,0:T(2,128)S(1)} %pad_maximum_fusion.21), channel_id=1, source_target_pairs={{0,4},{1,5},{2,6},{3,7},{8,12},{9,13},{10,14},{11,15},{16,20},{17,... | collective-permute-start | bytes 9224 | tf_op jit(solution)/shard_map/ppermute | solution.py:22
  169.5 4.3 %collective-permute-done.23 = f32[1,3,3,1,128]{4,3,2,1,0:T(1,128)S(1)} collective-permute-done((f32[1,3,3,1,128]{4,3,2,1,0:T(1,128)S(1)}, f32[1,3,3,1,128]{4,3,2,1,0:T(1,128)S(1)}, u32[]{:S(2)}, u32[]{:S(2)}) %collective-permute-start.23) | collective-permute-done | bytes 4640 | tf_op jit(solution)/shard_map/ppermute | solution.py:24
  181.2 2.6 maximum_dynamic-update-slice_fusion.1
  183.8 43.4 %all-reduce.1 = f32[64]{0:T(128)} all-reduce(f32[64]{0:T(128)} %maximum_dynamic-update-slice_fusion.1), channel_id=3, replica_groups=mesh['gx'=4,'gy'=2,'gz'=4] {'gx','gy','gz'}, use_global_device_ids=true, to_apply=%add.1 | all-reduce | flops 64 | bytes 512
  238.2 4.5 %collective-permute-start.24 = (f32[1,1,1,2,128]{4,3,2,1,0:T(2,128)S(1)}, f32[1,1,1,2,128]{4,3,2,1,0:T(2,128)S(1)}, u32[]{:S(2)}, u32[]{:S(2)}) collective-permute-start(f32[1,1,1,2,128]{4,3,2,1,0:T(2,128)S(1)} %bitcast.155), channel_id=1, source_target_pairs={{0,8},{8,16},{16,24},{1,9},{9,17},{17,25},{2,10},{10,18},{18,26},{... | collective-permute-start | bytes 3080 | tf_op jit(solution)/shard_map/ppermute | solution.py:22
  245.3 4.5 %collective-permute-start.26 = (f32[1,3,1,2,128]{4,3,2,1,0:T(2,128)S(1)}, f32[1,3,1,2,128]{4,3,2,1,0:T(2,128)S(1)}, u32[]{:S(2)}, u32[]{:S(2)}) collective-permute-start(f32[1,3,1,2,128]{4,3,2,1,0:T(2,128)S(1)} %pad_maximum_fusion.22), channel_id=1, source_target_pairs={{0,4},{1,5},{2,6},{3,7},{8,12},{9,13},{10,14},{11,15},{16,20},{17,... | collective-permute-start | bytes 9224 | tf_op jit(solution)/shard_map/ppermute | solution.py:22
  251.8 1.9 collective-permute-start.28
  272.4 44.9 %all-reduce.2 = f32[64]{0:T(128)S(1)} all-reduce(f32[64]{0:T(128)S(1)} %maximum_dynamic-update-slice_fusion.2), channel_id=4, replica_groups=mesh['gx'=4,'gy'=2,'gz'=4] {'gx','gy','gz'}, use_global_device_ids=true, to_apply=%add.2 | all-reduce | flops 64 | bytes 512
  325.6 3.1 multiply_reduce_fusion.1
  (219 shorter events, 105.4 us)
Async XLA Ops:
  2.7 7.6 %collective-permute-start.1 = (f32[7,1,1,2,128]{4,0,3,2,1:T(8,128)S(1)}, f32[7,1,1,2,128]{4,0,3,2,1:T(8,128)S(1)}, u32[]{:S(2)}, u32[]{:S(2)}) collective-permute-start(f32[7,1,1,2,128]{4,0,3,2,1:T(8,128)S(1)} %pad_maximum_fusion.19), channel_id=1, source_target_pairs={{8,0},{16,8},{24,16},{9,1},{17,9},{25,17},{10,2},{18,10},{26,18},{... | collective-permute-start | bytes 21512 | tf_op jit(solution)/shard_map/ppermute | solution.py:24
  4.0 6.9 %collective-permute-start = (f32[7,1,1,2,128]{4,0,3,2,1:T(8,128)S(1)}, f32[7,1,1,2,128]{4,0,3,2,1:T(8,128)S(1)}, u32[]{:S(2)}, u32[]{:S(2)}) collective-permute-start(f32[7,1,1,2,128]{4,0,3,2,1:T(8,128)S(1)} %pad_maximum_fusion.19), channel_id=1, source_target_pairs={{0,8},{8,16},{16,24},{1,9},{9,17},{17,25},{2,10},{10,18},{18,26},{... | collective-permute-start | bytes 21512 | tf_op jit(solution)/shard_map/ppermute | solution.py:22
  11.0 5.9 %collective-permute-start.3 = (f32[7,3,1,2,128]{4,0,3,2,1:T(8,128)S(1)}, f32[7,3,1,2,128]{4,0,3,2,1:T(8,128)S(1)}, u32[]{:S(2)}, u32[]{:S(2)}) collective-permute-start(f32[7,3,1,2,128]{4,0,3,2,1:T(8,128)S(1)} %pad_maximum_fusion.11), channel_id=1, source_target_pairs={{4,0},{5,1},{6,2},{7,3},{12,8},{13,9},{14,10},{15,11},{20,16},{21,... | collective-permute-start | bytes 64520 | tf_op jit(solution)/shard_map/ppermute | solution.py:24
  12.3 6.1 %collective-permute-start.2 = (f32[7,3,1,2,128]{4,0,3,2,1:T(8,128)S(1)}, f32[7,3,1,2,128]{4,0,3,2,1:T(8,128)S(1)}, u32[]{:S(2)}, u32[]{:S(2)}) collective-permute-start(f32[7,3,1,2,128]{4,0,3,2,1:T(8,128)S(1)} %pad_maximum_fusion.11), channel_id=1, source_target_pairs={{0,4},{1,5},{2,6},{3,7},{8,12},{9,13},{10,14},{11,15},{16,20},{17,... | collective-permute-start | bytes 64520 | tf_op jit(solution)/shard_map/ppermute | solution.py:22
  32.6 6.1 %collective-permute-start.7 = (f32[3,1,1,2,128]{4,3,0,2,1:T(2,128)S(1)}, f32[3,1,1,2,128]{4,3,0,2,1:T(2,128)S(1)}, u32[]{:S(2)}, u32[]{:S(2)}) collective-permute-start(f32[3,1,1,2,128]{4,3,0,2,1:T(2,128)S(1)} %bitcast.143), channel_id=1, source_target_pairs={{8,0},{16,8},{24,16},{9,1},{17,9},{25,17},{10,2},{18,10},{26,18},{... | collective-permute-start | bytes 9224 | tf_op jit(solution)/shard_map/ppermute | solution.py:24
  33.9 6.1 %collective-permute-start.6 = (f32[3,1,1,2,128]{4,3,0,2,1:T(2,128)S(1)}, f32[3,1,1,2,128]{4,3,0,2,1:T(2,128)S(1)}, u32[]{:S(2)}, u32[]{:S(2)}) collective-permute-start(f32[3,1,1,2,128]{4,3,0,2,1:T(2,128)S(1)} %bitcast.144), channel_id=1, source_target_pairs={{0,8},{8,16},{16,24},{1,9},{9,17},{17,25},{2,10},{10,18},{18,26},{... | collective-permute-start | bytes 9224 | tf_op jit(solution)/shard_map/ppermute | solution.py:22
  40.0 5.9 %collective-permute-start.9 = (f32[3,3,1,2,128]{4,3,0,2,1:T(2,128)S(1)}, f32[3,3,1,2,128]{4,3,0,2,1:T(2,128)S(1)}, u32[]{:S(2)}, u32[]{:S(2)}) collective-permute-start(f32[3,3,1,2,128]{4,3,0,2,1:T(2,128)S(1)} %pad_maximum_fusion.15), channel_id=1, source_target_pairs={{4,0},{5,1},{6,2},{7,3},{12,8},{13,9},{14,10},{15,11},{20,16},{21,... | collective-permute-start | bytes 27656 | tf_op jit(solution)/shard_map/ppermute | solution.py:24
  41.3 5.9 %collective-permute-start.8 = (f32[3,3,1,2,128]{4,3,0,2,1:T(2,128)S(1)}, f32[3,3,1,2,128]{4,3,0,2,1:T(2,128)S(1)}, u32[]{:S(2)}, u32[]{:S(2)}) collective-permute-start(f32[3,3,1,2,128]{4,3,0,2,1:T(2,128)S(1)} %pad_maximum_fusion.15), channel_id=1, source_target_pairs={{0,4},{1,5},{2,6},{3,7},{8,12},{9,13},{10,14},{11,15},{16,20},{17,... | collective-permute-start | bytes 27656 | tf_op jit(solution)/shard_map/ppermute | solution.py:22
  47.9 6.5 %collective-permute-start.11 = (f32[3,3,3,1,128]{4,3,0,2,1:T(1,128)}, f32[3,3,3,1,128]{4,3,0,2,1:T(1,128)}, u32[]{:S(2)}, u32[]{:S(2)}) collective-permute-start(f32[3,3,3,1,128]{4,3,0,2,1:T(1,128)} %get-tuple-element.27), channel_id=1, source_target_pairs={{1,0},{2,1},{3,2},{5,4},{6,5},{7,6},{9,8},{10,9},{11,10},{13,12},{... | collective-permute-start | bytes 41480 | tf_op jit(solution)/shard_map/ppermute | solution.py:24
  69.8 5.9 %collective-permute-start.13 = (f32[1,1,1,2,128]{4,3,2,1,0:T(2,128)S(1)}, f32[1,1,1,2,128]{4,3,2,1,0:T(2,128)S(1)}, u32[]{:S(2)}, u32[]{:S(2)}) collective-permute-start(f32[1,1,1,2,128]{4,3,2,1,0:T(2,128)S(1)} %bitcast.159), channel_id=1, source_target_pairs={{8,0},{16,8},{24,16},{9,1},{17,9},{25,17},{10,2},{18,10},{26,18},{... | collective-permute-start | bytes 3080 | tf_op jit(solution)/shard_map/ppermute | solution.py:24
  71.0 5.9 %collective-permute-start.12 = (f32[1,1,1,2,128]{4,3,2,1,0:T(2,128)S(1)}, f32[1,1,1,2,128]{4,3,2,1,0:T(2,128)S(1)}, u32[]{:S(2)}, u32[]{:S(2)}) collective-permute-start(f32[1,1,1,2,128]{4,3,2,1,0:T(2,128)S(1)} %bitcast.160), channel_id=1, source_target_pairs={{0,8},{8,16},{16,24},{1,9},{9,17},{17,25},{2,10},{10,18},{18,26},{... | collective-permute-start | bytes 3080 | tf_op jit(solution)/shard_map/ppermute | solution.py:22
  77.0 5.8 %collective-permute-start.15 = (f32[1,3,1,2,128]{4,3,2,1,0:T(2,128)S(1)}, f32[1,3,1,2,128]{4,3,2,1,0:T(2,128)S(1)}, u32[]{:S(2)}, u32[]{:S(2)}) collective-permute-start(f32[1,3,1,2,128]{4,3,2,1,0:T(2,128)S(1)} %pad_maximum_fusion.20), channel_id=1, source_target_pairs={{4,0},{5,1},{6,2},{7,3},{12,8},{13,9},{14,10},{15,11},{20,16},{21,... | collective-permute-start | bytes 9224 | tf_op jit(solution)/shard_map/ppermute | solution.py:24
  78.3 5.9 %collective-permute-start.14 = (f32[1,3,1,2,128]{4,3,2,1,0:T(2,128)S(1)}, f32[1,3,1,2,128]{4,3,2,1,0:T(2,128)S(1)}, u32[]{:S(2)}, u32[]{:S(2)}) collective-permute-start(f32[1,3,1,2,128]{4,3,2,1,0:T(2,128)S(1)} %pad_maximum_fusion.20), channel_id=1, source_target_pairs={{0,4},{1,5},{2,6},{3,7},{8,12},{9,13},{10,14},{11,15},{16,20},{17,... | collective-permute-start | bytes 9224 | tf_op jit(solution)/shard_map/ppermute | solution.py:22
  86.8 6.4 %collective-permute-start.17 = (f32[1,3,3,1,128]{4,3,2,1,0:T(1,128)}, f32[1,3,3,1,128]{4,3,2,1,0:T(1,128)}, u32[]{:S(2)}, u32[]{:S(2)}) collective-permute-start(f32[1,3,3,1,128]{4,3,2,1,0:T(1,128)} %get-tuple-element.40), channel_id=1, source_target_pairs={{1,0},{2,1},{3,2},{5,4},{6,5},{7,6},{9,8},{10,9},{11,10},{13,12},{... | collective-permute-start | bytes 13832 | tf_op jit(solution)/shard_map/ppermute | solution.py:24
  152.6 5.8 %collective-permute-start.19 = (f32[1,1,1,2,128]{4,3,2,1,0:T(2,128)S(1)}, f32[1,1,1,2,128]{4,3,2,1,0:T(2,128)S(1)}, u32[]{:S(2)}, u32[]{:S(2)}) collective-permute-start(f32[1,1,1,2,128]{4,3,2,1,0:T(2,128)S(1)} %bitcast.148), channel_id=1, source_target_pairs={{8,0},{16,8},{24,16},{9,1},{17,9},{25,17},{10,2},{18,10},{26,18},{... | collective-permute-start | bytes 3080 | tf_op jit(solution)/shard_map/ppermute | solution.py:24
  153.9 5.8 %collective-permute-start.18 = (f32[1,1,1,2,128]{4,3,2,1,0:T(2,128)S(1)}, f32[1,1,1,2,128]{4,3,2,1,0:T(2,128)S(1)}, u32[]{:S(2)}, u32[]{:S(2)}) collective-permute-start(f32[1,1,1,2,128]{4,3,2,1,0:T(2,128)S(1)} %bitcast.149), channel_id=1, source_target_pairs={{0,8},{8,16},{16,24},{1,9},{9,17},{17,25},{2,10},{10,18},{18,26},{... | collective-permute-start | bytes 3080 | tf_op jit(solution)/shard_map/ppermute | solution.py:22
  159.7 5.8 %collective-permute-start.21 = (f32[1,3,1,2,128]{4,3,2,1,0:T(2,128)S(1)}, f32[1,3,1,2,128]{4,3,2,1,0:T(2,128)S(1)}, u32[]{:S(2)}, u32[]{:S(2)}) collective-permute-start(f32[1,3,1,2,128]{4,3,2,1,0:T(2,128)S(1)} %pad_maximum_fusion.21), channel_id=1, source_target_pairs={{4,0},{5,1},{6,2},{7,3},{12,8},{13,9},{14,10},{15,11},{20,16},{21,... | collective-permute-start | bytes 9224 | tf_op jit(solution)/shard_map/ppermute | solution.py:24
  161.0 5.9 %collective-permute-start.20 = (f32[1,3,1,2,128]{4,3,2,1,0:T(2,128)S(1)}, f32[1,3,1,2,128]{4,3,2,1,0:T(2,128)S(1)}, u32[]{:S(2)}, u32[]{:S(2)}) collective-permute-start(f32[1,3,1,2,128]{4,3,2,1,0:T(2,128)S(1)} %pad_maximum_fusion.21), channel_id=1, source_target_pairs={{0,4},{1,5},{2,6},{3,7},{8,12},{9,13},{10,14},{11,15},{16,20},{17,... | collective-permute-start | bytes 9224 | tf_op jit(solution)/shard_map/ppermute | solution.py:22
  236.9 5.8 %collective-permute-start.25 = (f32[1,1,1,2,128]{4,3,2,1,0:T(2,128)S(1)}, f32[1,1,1,2,128]{4,3,2,1,0:T(2,128)S(1)}, u32[]{:S(2)}, u32[]{:S(2)}) collective-permute-start(f32[1,1,1,2,128]{4,3,2,1,0:T(2,128)S(1)} %bitcast.154), channel_id=1, source_target_pairs={{8,0},{16,8},{24,16},{9,1},{17,9},{25,17},{10,2},{18,10},{26,18},{... | collective-permute-start | bytes 3080 | tf_op jit(solution)/shard_map/ppermute | solution.py:24
  238.2 5.8 %collective-permute-start.24 = (f32[1,1,1,2,128]{4,3,2,1,0:T(2,128)S(1)}, f32[1,1,1,2,128]{4,3,2,1,0:T(2,128)S(1)}, u32[]{:S(2)}, u32[]{:S(2)}) collective-permute-start(f32[1,1,1,2,128]{4,3,2,1,0:T(2,128)S(1)} %bitcast.155), channel_id=1, source_target_pairs={{0,8},{8,16},{16,24},{1,9},{9,17},{17,25},{2,10},{10,18},{18,26},{... | collective-permute-start | bytes 3080 | tf_op jit(solution)/shard_map/ppermute | solution.py:22
  244.0 5.8 %collective-permute-start.27 = (f32[1,3,1,2,128]{4,3,2,1,0:T(2,128)S(1)}, f32[1,3,1,2,128]{4,3,2,1,0:T(2,128)S(1)}, u32[]{:S(2)}, u32[]{:S(2)}) collective-permute-start(f32[1,3,1,2,128]{4,3,2,1,0:T(2,128)S(1)} %pad_maximum_fusion.22), channel_id=1, source_target_pairs={{4,0},{5,1},{6,2},{7,3},{12,8},{13,9},{14,10},{15,11},{20,16},{21,... | collective-permute-start | bytes 9224 | tf_op jit(solution)/shard_map/ppermute | solution.py:24
  245.3 5.9 %collective-permute-start.26 = (f32[1,3,1,2,128]{4,3,2,1,0:T(2,128)S(1)}, f32[1,3,1,2,128]{4,3,2,1,0:T(2,128)S(1)}, u32[]{:S(2)}, u32[]{:S(2)}) collective-permute-start(f32[1,3,1,2,128]{4,3,2,1,0:T(2,128)S(1)} %pad_maximum_fusion.22), channel_id=1, source_target_pairs={{0,4},{1,5},{2,6},{3,7},{8,12},{9,13},{10,14},{11,15},{16,20},{17,... | collective-permute-start | bytes 9224 | tf_op jit(solution)/shard_map/ppermute | solution.py:22
  251.8 8.7 %collective-permute-start.28 = (f32[1,3,3,1,128]{4,3,2,1,0:T(1,128)}, f32[1,3,3,1,128]{4,3,2,1,0:T(1,128)}, u32[]{:S(2)}, u32[]{:S(2)}) collective-permute-start(f32[1,3,3,1,128]{4,3,2,1,0:T(1,128)} %get-tuple-element.31), channel_id=1, source_target_pairs={{0,1},{1,2},{2,3},{4,5},{5,6},{6,7},{8,9},{9,10},{10,11},{12,13},{... | collective-permute-start | bytes 13832 | tf_op jit(solution)/shard_map/ppermute | solution.py:22
  253.7 6.8 %collective-permute-start.29 = (f32[1,3,3,1,128]{4,3,2,1,0:T(1,128)}, f32[1,3,3,1,128]{4,3,2,1,0:T(1,128)}, u32[]{:S(2)}, u32[]{:S(2)}) collective-permute-start(f32[1,3,3,1,128]{4,3,2,1,0:T(1,128)} %get-tuple-element.32), channel_id=1, source_target_pairs={{1,0},{2,1},{3,2},{5,4},{6,5},{7,6},{9,8},{10,9},{11,10},{13,12},{... | collective-permute-start | bytes 13832 | tf_op jit(solution)/shard_map/ppermute | solution.py:24
  (45 other events, 670.1 us)
